TPU v7x, 256 devices: a whole 4x4x8 slice. The times are simulated.
256 devices in a mesh: tile: 16 (over y, z_hi), spec: 16 (over x, z_lo, core).
Axes of the slice: x: 4, y: 4, z: 8 (z_hi: 4, z_lo: 2; z = z_hi * 2 + z_lo), core: 2. Of those that a mesh axis runs over, the one named last changes fastest.
Arguments:
- latent: bfloat16 [32, 4096, 1024], P(None, ('tile', 'spec')), may hold values from -6 to 6
- basis: bfloat16 [224, 32], replicated, may hold values from -1 to 1
- response: bfloat16 [8, 224], replicated, may hold values from -0.375 to 0.375
- hyper_obs: bfloat16 [224, 1024, 256], P('spec', 'tile'), may hold values from -6 to 6
- multi_obs: bfloat16 [8, 4096, 1024], P(None, ('tile', 'spec')), may hold values from -6 to 6
Outputs:
- z_next: bfloat16 [32, 4096, 1024], P(None, ('tile', 'spec'))
- hs_residual: bfloat16 [224, 1024, 256], P('spec', 'tile')
All inputs are finite; a program needn't handle non-finite values.
Results may differ from a plain program's by a relative error of at most 0.0054.
Values may be sent and summed in bfloat16 or wider, within the bound.
No kernel may reach another device: no remote copies, remote signals or barrier semaphores. Data moves between devices by JAX's collectives and lax.ppermute only.
A program may use at most 128 MiB of HBM per device.

v0:
```python
import jax
import jax.numpy as jnp
from jax import lax
from jax.sharding import PartitionSpec as P

DECIM = 4
HALO = 128
step_size = 0.3


def with_halo(cells, sides, width):
    for axis, dim in sides:
        count = lax.axis_size(axis)
        ends = count - 1
        head = lax.slice_in_dim(cells, 0, width, axis=dim)
        tail = lax.slice_in_dim(cells, cells.shape[dim] - width, cells.shape[dim], axis=dim)
        cells = jnp.concatenate(
            [
                lax.ppermute(tail, axis, [(i, (i + 1) % count) for i in range(ends)]),
                cells,
                lax.ppermute(head, axis, [((i + 1) % count, i) for i in range(ends)]),
            ],
            axis=dim,
        )
    return cells


def profile(where_at):
    narrow = DECIM / 2.0
    decay_len = 3.0 * HALO / 8.0
    ripple = jnp.cos(where_at * (jnp.pi / 7.0))
    return (
        jnp.exp(-where_at * where_at / (2.0 * narrow * narrow))
        + 0.5 * jnp.exp(-jnp.abs(where_at) / decay_len) * ripple * ripple
    )


def kernel_values(offsets):
    every_offset = jnp.arange(-HALO, HALO + 1).astype(jnp.float32)
    energy = jnp.sqrt(jnp.sum(profile(every_offset) ** 2))
    inside = jnp.abs(offsets) <= HALO
    return jnp.where(inside, profile(offsets.astype(jnp.float32)) / energy, 0.0).astype(
        jnp.bfloat16
    )


def column_matrix(fine_count, coarse_count):
    fine_cols = jnp.arange(fine_count)[:, None]
    coarse = jnp.arange(coarse_count)[None, :]
    return kernel_values(fine_cols - DECIM * coarse)


def row_matrix(rows_local):
    coarse = jnp.arange(rows_local // DECIM)[:, None]
    padded = jnp.arange(rows_local + 2 * HALO)[None, :]
    return kernel_values(padded - HALO - DECIM * coarse)


def back_matrix(rows_local):
    fine_rows = jnp.arange(rows_local)[:, None]
    coarse = jnp.arange(rows_local // DECIM + 2 * (HALO // DECIM))[None, :]
    return kernel_values(fine_rows - DECIM * coarse + HALO)


def shards(latent, basis, response, hyper_obs, multi_obs):
    highest = lax.Precision.HIGHEST
    rows_dev = hyper_obs.shape[1] * DECIM
    width_cols = latent.shape[2]
    spectra = jnp.einsum("bk,krc->brc", basis, latent, preferred_element_type=jnp.float32).astype(
        jnp.bfloat16
    )
    column_kernel = column_matrix(width_cols, width_cols // DECIM)
    column_wide = column_kernel.astype(jnp.float32)
    band_cube = lax.all_to_all(spectra, "spec", split_axis=0, concat_axis=1, tiled=True)
    padded = with_halo(band_cube, (("tile", 1),), HALO)
    rows_done = jnp.einsum(
        "ir,brc->bic", row_matrix(rows_dev), padded, preferred_element_type=jnp.float32
    )
    blurred = jnp.einsum("bic,cj->bij", rows_done, column_wide, precision=highest)
    hs_residual = (blurred - hyper_obs.astype(jnp.float32)).astype(jnp.bfloat16)
    coarse_padded = with_halo(hs_residual, (("tile", 1),), HALO // DECIM)
    rows_back = jnp.einsum(
        "rq,bqj->brj", back_matrix(rows_dev), coarse_padded, preferred_element_type=jnp.float32
    )
    multi_resid = (
        jnp.einsum("mb,brc->mrc", response, spectra, preferred_element_type=jnp.float32)
        - multi_obs.astype(jnp.float32)
    ).astype(jnp.bfloat16)
    spread = jnp.einsum("brj,cj->brc", rows_back, column_wide, precision=highest).astype(
        jnp.bfloat16
    )
    spread_pixel = lax.all_to_all(spread, "spec", split_axis=1, concat_axis=0, tiled=True)
    multi_back = jnp.einsum(
        "mb,mrc->brc", response, multi_resid, preferred_element_type=jnp.float32
    )
    spectral = (spread_pixel.astype(jnp.float32) + multi_back).astype(jnp.bfloat16)
    gradient = jnp.einsum("bk,brc->krc", basis, spectral, preferred_element_type=jnp.float32)
    z_next = (latent.astype(jnp.float32) - step_size * gradient).astype(jnp.bfloat16)
    return (z_next, hs_residual)


def solution(mesh):
    in_specs = (
        P(None, ("tile", "spec"), None),
        P(),
        P(),
        P("spec", "tile", None),
        P(None, ("tile", "spec"), None),
    )
    out_specs = (P(None, ("tile", "spec"), None), P("spec", "tile", None))
    return jax.shard_map(shards, mesh=mesh, in_specs=in_specs, out_specs=out_specs, check_vma=False)
```

profile of v0, /device:TPU:16, one launch (start us, length us, event | category | flops | bytes accessed | tf_op | source)
XLA Modules:
  0.0 485.2 jit_solution(12088717307099178395)
XLA Ops:
  1.4 3.3 convolution_convert_fusion.1
  4.7 7.1 %copy.30 = bf16[224,16,1024]{2,1,0:T(8,128)(2,1)} copy(bf16[224,16,1024]{2,0,1:T(8,128)(2,1)S(1)} %convolution_convert_fusion.1) | data formatting | bytes 14680064 | tf_op jit(solution)/shard_map/convert_element_type | solution.py:69
  11.8 89.8 %all_to_all.27 = bf16[224,16,1024]{2,1,0:T(8,128)(2,1)} all-to-all(bf16[224,16,1024]{2,1,0:T(8,128)(2,1)} %copy.30), channel_id=1, replica_groups=mesh['tile'=16,'spec'=16] {'spec'}, dimensions={0} | all-to-all | bytes 14680064 | tf_op jit(solution)/shard_map/all_to_all | solution.py:74
  101.6 4.7 copy.31
  106.3 4.8 fusion.119
  112.0 5.2 %collective-permute-start = (bf16[14,128,1024]{2,1,0:T(8,128)(2,1)}, bf16[14,128,1024]{2,1,0:T(8,128)(2,1)}, u32[]{:S(2)}, u32[]{:S(2)}) collective-permute-start(bf16[14,128,1024]{2,1,0:T(8,128)(2,1)} %get-tuple-element.10), channel_id=1, source_target_pairs={{0,16},{16,32},{32,48},{48,64},{64,80},{80,96},{96,112},{112,128},... | collective-permute-start | bytes 11010056 | tf_op jit(solution)/shard_map/ppermute | solution.py:19
  117.2 4.1 collective-permute-start.1
  122.7 76.3 %collective-permute-done = bf16[14,128,1024]{2,1,0:T(8,128)(2,1)} collective-permute-done((bf16[14,128,1024]{2,1,0:T(8,128)(2,1)}, bf16[14,128,1024]{2,1,0:T(8,128)(2,1)}, u32[]{:S(2)}, u32[]{:S(2)}) %collective-permute-start) | collective-permute-done | bytes 3670048 | tf_op jit(solution)/shard_map/ppermute | solution.py:19
  199.0 64.5 %collective-permute-done.1 = bf16[14,128,1024]{2,1,0:T(8,128)(2,1)} collective-permute-done((bf16[14,128,1024]{2,1,0:T(8,128)(2,1)}, bf16[14,128,1024]{2,1,0:T(8,128)(2,1)}, u32[]{:S(2)}, u32[]{:S(2)}) %collective-permute-start.1) | collective-permute-done | bytes 3670048 | tf_op jit(solution)/shard_map/ppermute | solution.py:21
  263.5 8.2 %fusion = f32[14,1024,64]{1,2,0:T(8,128)S(1)} fusion(bf16[14,128,1024]{2,1,0:T(8,128)(2,1)} %collective-permute-done.1, bf16[14,256,1024]{2,1,0:T(8,128)(2,1)} %bitcast.62, bf16[14,128,1024]{2,1,0:T(8,128)(2,1)} %collective-permute-done, f32[]{:T(128)S(6)} %sqrt.2, s32[64]{0:T(128)S(1)} %iota_multiply_fusion.2, s32[512]{0:T(512)S(1)} %iota_add_fusion), kind=kOutput, calls=%fused_computation | convolution fusion | flops 984154112 | bytes 18352388 | tf_op jit(solution)/shard_map/ir,brc->bic/dot_general | solution.py:76
  271.7 5.9 %fusion.15 = bf16[14,64,256]{2,1,0:T(8,128)(2,1)S(1)} fusion(f32[14,1024,64]{1,2,0:T(8,128)S(1)} %fusion, bf16[14,64,256]{2,1,0:T(8,128)(2,1)S(1)} %copy-done.7, f32[]{:T(128)S(6)} %sqrt.2, s32[256]{0:T(256)S(1)} %iota_multiply_fusion), kind=kOutput, calls=%fused_computation.20 | convolution fusion | flops 2823979008 | bytes 4588548 | tf_op jit(solution)/shard_map/bic,cj->bij/dot_general | solution.py:79
  277.7 23.1 %collective-permute-start.2 = (bf16[14,32,256]{2,1,0:T(8,128)(2,1)S(1)}, bf16[14,32,256]{2,1,0:T(8,128)(2,1)S(1)}, u32[]{:S(2)}, u32[]{:S(2)}) collective-permute-start(bf16[14,32,256]{2,1,0:T(8,128)(2,1)S(1)} %get-tuple-element.12), channel_id=1, source_target_pairs={{0,16},{16,32},{32,48},{48,64},{64,80},{80,96},{96,112},{112,128},... | collective-permute-start | bytes 688136 | tf_op jit(solution)/shard_map/ppermute | solution.py:19
  300.8 2.1 collective-permute-start.3
  303.0 5.4 %collective-permute-done.2 = bf16[14,32,256]{2,1,0:T(8,128)(2,1)S(1)} collective-permute-done((bf16[14,32,256]{2,1,0:T(8,128)(2,1)S(1)}, bf16[14,32,256]{2,1,0:T(8,128)(2,1)S(1)}, u32[]{:S(2)}, u32[]{:S(2)}) %collective-permute-start.2) | collective-permute-done | bytes 229408 | tf_op jit(solution)/shard_map/ppermute | solution.py:19
  308.4 4.7 collective-permute-done.3
  314.3 16.4 %convolution_convert_fusion = bf16[14,256,1024]{2,1,0:T(8,128)(2,1)S(1)} fusion(f32[14,256,256]{2,1,0:T(8,128)S(1)} %fusion.27, f32[]{:T(128)S(6)} %sqrt.2, s32[256]{0:T(256)S(1)} %iota_multiply_fusion), kind=kOutput, calls=%fused_computation.9 | convolution fusion | flops 11282677760 | bytes 11011076 | tf_op jit(solution)/shard_map/brj,cj->brc/dot_general | solution.py:89
  330.7 7.5 %copy.34 = bf16[14,256,1024]{2,0,1:T(8,128)(2,1)} copy(bf16[14,256,1024]{2,1,0:T(8,128)(2,1)S(1)} %convolution_convert_fusion) | data formatting | bytes 14680064 | tf_op jit(solution)/shard_map/convert_element_type | solution.py:89
  338.2 5.3 %all-to-all-start.1 = ((bf16[14,256,1024]{2,0,1:T(8,128)(2,1)}), bf16[14,256,1024]{2,0,1:T(8,128)(2,1)}, u32[]{:S(2)}, u32[]{:S(2)}) async-start(bf16[14,256,1024]{2,0,1:T(8,128)(2,1)} %copy.34), calls=%async_computation.1 | async-start | bytes 16777216 | tf_op jit(solution)/shard_map/all_to_all | solution.py:92
  343.5 5.0 %fusion.19 = bf16[8,16,1024]{2,0,1:T(8,128)(2,1)S(1)} fusion(bf16[224,16,1024]{2,0,1:T(8,128)(2,1)} %copy-done.1, bf16[8,16,1024]{2,1,0:T(8,128)(2,1)S(1)} %copy-done.5, bf16[8,224]{1,0:T(8,128)(2,1)S(1)} %copy-done.6), kind=kOutput, calls=%fused_computation.23 | convolution fusion | flops 59113472 | bytes 7867904 | tf_op jit(solution)/shard_map/mb,brc->mrc/dot_general | solution.py:86
  348.5 89.9 %all-to-all-done.1 = bf16[14,256,1024]{2,0,1:T(8,128)(2,1)} async-done(((bf16[14,256,1024]{2,0,1:T(8,128)(2,1)}), bf16[14,256,1024]{2,0,1:T(8,128)(2,1)}, u32[]{:S(2)}, u32[]{:S(2)}) %all-to-all-start.1) | async-done | bytes 7340064 | tf_op jit(solution)/shard_map/all_to_all | solution.py:92
  438.4 7.5 %copy.35 = bf16[14,256,1024]{2,1,0:T(8,128)(2,1)S(1)} copy(bf16[14,256,1024]{2,0,1:T(8,128)(2,1)} %all-to-all-done.1) | data formatting | bytes 14680064 | tf_op jit(solution)/shard_map/all_to_all | solution.py:92
  445.9 7.1 %convert_bitcast_fusion = f32[16,14,16,1024]{3,2,0,1:T(8,128)} fusion(bf16[14,16,16,1024]{3,2,1,0:T(8,128)(2,1)S(1)} %bitcast.64), kind=kLoop, calls=%fused_computation.6 | loop fusion | flops 3670016 | bytes 22020096 | tf_op jit(solution)/shard_map/convert_element_type | solution.py:96
  453.0 13.7 %copy.36 = f32[16,14,16,1024]{3,2,1,0:T(8,128)} copy(f32[16,14,16,1024]{3,2,0,1:T(8,128)} %convert_bitcast_fusion) | data formatting | bytes 29360128 | tf_op jit(solution)/shard_map/convert_element_type | solution.py:96
  466.7 16.8 %fusion.11 = bf16[32,16,1024]{2,0,1:T(8,128)(2,1)S(1)} fusion(f32[224,16,1024]{2,1,0:T(8,128)} %bitcast.60, bf16[8,16,1024]{2,0,1:T(8,128)(2,1)S(1)} %fusion.19, bf16[32,16,1024]{2,1,0:T(8,128)(2,1)S(1)} %copy-done.3, bf16[224,32]{0,1:T(8,128)(2,1)S(1)} %copy-done, bf16[8,224]{1,0:T(8,128)(2,1)S(1)} %copy-done.6), kind=kOutput, calls=%fused_computation.16 | convolution fusion | flops 303038464 | bytes 17057280 | tf_op jit(solution)/shard_map/bk,brc->krc/dot_general | solution.py:97
  (24 shorter events, 5.0 us)
Async XLA Ops:
  0.6 0.7 copy-start
  4.7 7.1 %copy-start.1 = (bf16[224,16,1024]{2,0,1:T(8,128)(2,1)}, bf16[224,16,1024]{2,0,1:T(8,128)(2,1)S(1)}, u32[]{:S(2)}) copy-start(bf16[224,16,1024]{2,0,1:T(8,128)(2,1)S(1)} %convolution_convert_fusion.1) | copy-start | bytes 22020100
  106.3 5.7 %copy-start.2 = (bf16[14,16,16,1024]{3,2,1,0:T(8,128)(2,1)}, bf16[14,16,16,1024]{3,2,1,0:T(8,128)(2,1)S(1)}, u32[]{:S(2)}) copy-start(bf16[14,16,16,1024]{3,2,1,0:T(8,128)(2,1)S(1)} %copy.31) | copy-start | bytes 22020100
  112.0 87.0 %collective-permute-start = (bf16[14,128,1024]{2,1,0:T(8,128)(2,1)}, bf16[14,128,1024]{2,1,0:T(8,128)(2,1)}, u32[]{:S(2)}, u32[]{:S(2)}) collective-permute-start(bf16[14,128,1024]{2,1,0:T(8,128)(2,1)} %get-tuple-element.10), channel_id=1, source_target_pairs={{0,16},{16,32},{32,48},{48,64},{64,80},{80,96},{96,112},{112,128},... | collective-permute-start | bytes 11010056 | tf_op jit(solution)/shard_map/ppermute | solution.py:19
  117.2 146.4 %collective-permute-start.1 = (bf16[14,128,1024]{2,1,0:T(8,128)(2,1)}, bf16[14,128,1024]{2,1,0:T(8,128)(2,1)}, u32[]{:S(2)}, u32[]{:S(2)}) collective-permute-start(bf16[14,128,1024]{2,1,0:T(8,128)(2,1)} %get-tuple-element.11), channel_id=1, source_target_pairs={{16,0},{32,16},{48,32},{64,48},{80,64},{96,80},{112,96},{128,112},... | collective-permute-start | bytes 11010056 | tf_op jit(solution)/shard_map/ppermute | solution.py:21
  122.7 149.1 %copy-start.7 = (bf16[14,64,256]{2,1,0:T(8,128)(2,1)S(1)}, bf16[14,64,256]{2,1,0:T(8,128)(2,1)}, u32[]{:S(2)}) copy-start(bf16[14,64,256]{2,1,0:T(8,128)(2,1)} %param.8) | copy-start | bytes 1376260
  277.7 53.0 %copy-start.4 = (bf16[14,64,256]{2,1,0:T(8,128)(2,1)}, bf16[14,64,256]{2,1,0:T(8,128)(2,1)S(1)}, u32[]{:S(2)}) copy-start(bf16[14,64,256]{2,1,0:T(8,128)(2,1)S(1)} %fusion.15) | copy-start | bytes 1376260
  277.7 30.7 %collective-permute-start.2 = (bf16[14,32,256]{2,1,0:T(8,128)(2,1)S(1)}, bf16[14,32,256]{2,1,0:T(8,128)(2,1)S(1)}, u32[]{:S(2)}, u32[]{:S(2)}) collective-permute-start(bf16[14,32,256]{2,1,0:T(8,128)(2,1)S(1)} %get-tuple-element.12), channel_id=1, source_target_pairs={{0,16},{16,32},{32,48},{48,64},{64,80},{80,96},{96,112},{112,128},... | collective-permute-start | bytes 688136 | tf_op jit(solution)/shard_map/ppermute | solution.py:19
  300.8 12.3 %collective-permute-start.3 = (bf16[14,32,256]{2,1,0:T(8,128)(2,1)S(1)}, bf16[14,32,256]{2,1,0:T(8,128)(2,1)S(1)}, u32[]{:S(2)}, u32[]{:S(2)}) collective-permute-start(bf16[14,32,256]{2,1,0:T(8,128)(2,1)S(1)} %get-tuple-element.13), channel_id=1, source_target_pairs={{16,0},{32,16},{48,32},{64,48},{80,64},{96,80},{112,96},{128,112},... | collective-permute-start | bytes 688136 | tf_op jit(solution)/shard_map/ppermute | solution.py:21
  338.2 5.3 %copy-start.5 = (bf16[8,16,1024]{2,1,0:T(8,128)(2,1)S(1)}, bf16[8,16,1024]{2,1,0:T(8,128)(2,1)}, u32[]{:S(2)}) copy-start(bf16[8,16,1024]{2,1,0:T(8,128)(2,1)} %param.9) | copy-start | bytes 786436
  338.2 5.3 %copy-start.6 = (bf16[8,224]{1,0:T(8,128)(2,1)S(1)}, bf16[8,224]{1,0:T(8,128)(2,1)}, u32[]{:S(2)}) copy-start(bf16[8,224]{1,0:T(8,128)(2,1)} %param.7) | copy-start | bytes 10756
  338.2 100.2 %all-to-all-start.1 = ((bf16[14,256,1024]{2,0,1:T(8,128)(2,1)}), bf16[14,256,1024]{2,0,1:T(8,128)(2,1)}, u32[]{:S(2)}, u32[]{:S(2)}) async-start(bf16[14,256,1024]{2,0,1:T(8,128)(2,1)} %copy.34), calls=%async_computation.1 | async-start | bytes 16777216 | tf_op jit(solution)/shard_map/all_to_all | solution.py:92
  453.0 13.7 %copy-start.3 = (bf16[32,16,1024]{2,1,0:T(8,128)(2,1)S(1)}, bf16[32,16,1024]{2,1,0:T(8,128)(2,1)}, u32[]{:S(2)}) copy-start(bf16[32,16,1024]{2,1,0:T(8,128)(2,1)} %param.5) | copy-start | bytes 3145732
where the time goes:
time: 492 us; the launch traced here: 485 us
  waiting for transfers between devices  241 us (49%)
  blocking collectives  89.8 us (18%)
  matrix products  56.8 us (12%)
  local copies, waits for them, and re-layouts  48.5 us (10%)
  starting transfers between devices  39.8 us (8%)
  other arithmetic  7.76 us (2%)
    all_to_all x1, waiting for transfers between devices, shards(): lax.all_to_all(spread, 'spec', split_axis=1, concat_axis=0, tiled=True)  89.9 us
    all_to_all x1, blocking collectives, shards(): lax.all_to_all(spectra, 'spec', split_axis=0, concat_axis=1, tiled=True)  89.8 us
    ppermute x2, waiting for transfers between devices, with_halo(): lax.ppermute(tail, axis, [(i, (i + 1) % count) for i in range(ends)])  81.8 us
    ppermute x2, waiting for transfers between devices, with_halo(): lax.ppermute(head, axis, [((i + 1) % count, i) for i in range(ends)])  69.2 us
    ppermute x2, starting transfers between devices, with_halo(): lax.ppermute(tail, axis, [(i, (i + 1) % count) for i in range(ends)])  28.2 us
    dot_general x1, matrix products, shards(): jnp.einsum('bk,brc->krc', basis, spectral, preferred_element_type=jnp.flo...  16.8 us
    dot_general x1, matrix products, shards(): jnp.einsum('brj,cj->brc', rows_back, column_wide, precision=highest)  16.4 us
    convert_element_type x1, local copies, waits for them, and re-layouts, shards(): spread_pixel.astype(jnp.float32) + multi_back  13.7 us
  transfers between devices with their start and end apart: 5, of which 5 were waited for; matrix products, arithmetic and copies ran while one was open for 1% of the time, Pallas kernels for 0%

commit v1 on v0

--- a/solution.py
+++ b/solution.py
@@ -63,6 +63,13 @@
 
 
 def shards(latent, basis, response, hyper_obs, multi_obs):
+
+    def bring_axis_part(inp, named_axis):
+        x_new = lax.axis_size(named_axis)
+        answer = jnp.split(inp, x_new, axis=0)
+        last = lax.all_to_all(jnp.stack(answer), named_axis, split_axis=0, concat_axis=0)
+        return jnp.concatenate(last, axis=1)
+
     highest = lax.Precision.HIGHEST
     rows_dev = hyper_obs.shape[1] * DECIM
     width_cols = latent.shape[2]
@@ -71,7 +78,7 @@
     )
     column_kernel = column_matrix(width_cols, width_cols // DECIM)
     column_wide = column_kernel.astype(jnp.float32)
-    band_cube = lax.all_to_all(spectra, "spec", split_axis=0, concat_axis=1, tiled=True)
+    band_cube = bring_axis_part(spectra, "spec")
     padded = with_halo(band_cube, (("tile", 1),), HALO)
     rows_done = jnp.einsum(
         "ir,brc->bic", row_matrix(rows_dev), padded, preferred_element_type=jnp.float32

time: 492 us -> 512 us (1.041)
  local copies, waits for them, and re-layouts: 48.5 us -> 67.5 us
  waiting for transfers between devices: 241 us -> 253 us
  starting transfers between devices: 39.8 us -> 27.8 us
    unnamed x17 -> x32, local copies, waits for them, and re-layouts: 3.15 us -> 20.5 us
    ppermute x2, starting transfers between devices: 28.2 us -> 16.5 us  [with_halo(): lax.ppermute(tail, axis, [(i, (i + 1) % count) for i in range(ends)])]
    ppermute x2, waiting for transfers between devices: 69.2 us -> 80.8 us  [with_halo(): lax.ppermute(head, axis, [((i + 1) % count, i) for i in range(ends)])]
    another operation x0 -> x2, local copies, waits for them, and re-layouts: none -> 9.23 us  [bring_axis_part(): jnp.stack(answer)]
    convert_element_type x1 -> x0, local copies, waits for them, and re-layouts: 7.11 us -> none  [shards(): jnp.einsum('bk,krc->brc', basis, latent, preferred_element_type=jnp.float32)]
where the time goes in v1:
time: 512 us; the launch traced here: 504 us
  waiting for transfers between devices  253 us (49%)
  blocking collectives  89.7 us (18%)
  local copies, waits for them, and re-layouts  67.5 us (13%)
  matrix products  56.8 us (11%)
  starting transfers between devices  27.8 us (5%)
  other arithmetic  7.76 us (2%)
    all_to_all x1, waiting for transfers between devices, shards(): lax.all_to_all(spread, 'spec', split_axis=1, concat_axis=0, tiled=True)  89.9 us
    all_to_all x1, blocking collectives, bring_axis_part(): lax.all_to_all(jnp.stack(answer), named_axis, split_axis=0, concat_axis=0)  89.7 us
    ppermute x2, waiting for transfers between devices, with_halo(): lax.ppermute(tail, axis, [(i, (i + 1) % count) for i in range(ends)])  81.9 us
    ppermute x2, waiting for transfers between devices, with_halo(): lax.ppermute(head, axis, [((i + 1) % count, i) for i in range(ends)])  80.8 us
    unnamed x32, local copies, waits for them, and re-layouts  20.5 us
    dot_general x1, matrix products, shards(): jnp.einsum('bk,brc->krc', basis, spectral, preferred_element_type=jnp.flo...  16.8 us
    ppermute x2, starting transfers between devices, with_halo(): lax.ppermute(tail, axis, [(i, (i + 1) % count) for i in range(ends)])  16.5 us
    dot_general x1, matrix products, shards(): jnp.einsum('brj,cj->brc', rows_back, column_wide, precision=highest)  16.4 us
  transfers between devices with their start and end apart: 5, of which 5 were waited for; matrix products, arithmetic and copies ran while one was open for 1% of the time, Pallas kernels for 0%

profile of v1, /device:TPU:16, one launch (start us, length us, event | category | flops | bytes accessed | tf_op | source)
XLA Modules:
  0.0 504.0 jit_solution(15301786171406721684)
XLA Ops:
  1.4 3.3 convolution_convert_fusion.1
  20.9 8.3 %copy.28 = bf16[16,14,16,1024]{3,2,1,0:T(8,128)(2,1)S(1)} copy(bf16[16,14,16,1024]{3,1,2,0:T(8,128)(2,1)} %fusion.34) | data formatting | bytes 14680064 | tf_op jit(solution)/shard_map/stack | solution.py:70
  29.2 89.7 %all_to_all.14 = bf16[16,14,16,1024]{3,2,1,0:T(8,128)(2,1)} all-to-all(bf16[16,14,16,1024]{3,2,1,0:T(8,128)(2,1)S(1)} %copy.28), channel_id=1, replica_groups=mesh['tile'=16,'spec'=16] {'spec'}, dimensions={0} | all-to-all | bytes 14680064 | tf_op jit(solution)/shard_map/all_to_all | solution.py:70
  118.9 4.7 copy.29
  123.6 3.0 copy-done.2
  126.6 4.3 fusion.135
  131.0 5.2 %collective-permute-start = (bf16[14,128,1024]{2,1,0:T(8,128)(2,1)}, bf16[14,128,1024]{2,1,0:T(8,128)(2,1)}, u32[]{:S(2)}, u32[]{:S(2)}) collective-permute-start(bf16[14,128,1024]{2,1,0:T(8,128)(2,1)} %get-tuple-element.10), channel_id=1, source_target_pairs={{0,16},{16,32},{32,48},{48,64},{64,80},{80,96},{96,112},{112,128},... | collective-permute-start | bytes 11010056 | tf_op jit(solution)/shard_map/ppermute | solution.py:19
  136.1 3.9 collective-permute-start.1
  141.5 76.5 %collective-permute-done = bf16[14,128,1024]{2,1,0:T(8,128)(2,1)} collective-permute-done((bf16[14,128,1024]{2,1,0:T(8,128)(2,1)}, bf16[14,128,1024]{2,1,0:T(8,128)(2,1)}, u32[]{:S(2)}, u32[]{:S(2)}) %collective-permute-start) | collective-permute-done | bytes 3670048 | tf_op jit(solution)/shard_map/ppermute | solution.py:19
  218.0 76.1 %collective-permute-done.1 = bf16[14,128,1024]{2,1,0:T(8,128)(2,1)} collective-permute-done((bf16[14,128,1024]{2,1,0:T(8,128)(2,1)}, bf16[14,128,1024]{2,1,0:T(8,128)(2,1)}, u32[]{:S(2)}, u32[]{:S(2)}) %collective-permute-start.1) | collective-permute-done | bytes 3670048 | tf_op jit(solution)/shard_map/ppermute | solution.py:21
  294.1 8.2 %fusion = f32[14,1024,64]{1,2,0:T(8,128)S(1)} fusion(bf16[14,128,1024]{2,1,0:T(8,128)(2,1)} %collective-permute-done.1, bf16[14,256,1024]{2,1,0:T(8,128)(2,1)} %bitcast.124, bf16[14,128,1024]{2,1,0:T(8,128)(2,1)} %collective-permute-done, f32[]{:T(128)S(6)} %sqrt.2, s32[64]{0:T(128)S(1)} %iota_multiply_fusion.2, s32[512]{0:T(512)S(1)} %iota_add_fusion), kind=kOutput, calls=%fused_computation | convolution fusion | flops 984154112 | bytes 18352388 | tf_op jit(solution)/shard_map/ir,brc->bic/dot_general | solution.py:83
  302.3 5.9 %fusion.15 = bf16[14,64,256]{2,1,0:T(8,128)(2,1)S(1)} fusion(f32[14,1024,64]{1,2,0:T(8,128)S(1)} %fusion, bf16[14,64,256]{2,1,0:T(8,128)(2,1)S(1)} %copy-done.7, f32[]{:T(128)S(6)} %sqrt.2, s32[256]{0:T(256)S(1)} %iota_multiply_fusion), kind=kOutput, calls=%fused_computation.20 | convolution fusion | flops 2823979008 | bytes 4588548 | tf_op jit(solution)/shard_map/bic,cj->bij/dot_general | solution.py:86
  308.3 11.3 %collective-permute-start.2 = (bf16[14,32,256]{2,1,0:T(8,128)(2,1)S(1)}, bf16[14,32,256]{2,1,0:T(8,128)(2,1)S(1)}, u32[]{:S(2)}, u32[]{:S(2)}) collective-permute-start(bf16[14,32,256]{2,1,0:T(8,128)(2,1)S(1)} %get-tuple-element.12), channel_id=1, source_target_pairs={{0,16},{16,32},{32,48},{48,64},{64,80},{80,96},{96,112},{112,128},... | collective-permute-start | bytes 688136 | tf_op jit(solution)/shard_map/ppermute | solution.py:19
  321.8 5.4 %collective-permute-done.2 = bf16[14,32,256]{2,1,0:T(8,128)(2,1)S(1)} collective-permute-done((bf16[14,32,256]{2,1,0:T(8,128)(2,1)S(1)}, bf16[14,32,256]{2,1,0:T(8,128)(2,1)S(1)}, u32[]{:S(2)}, u32[]{:S(2)}) %collective-permute-start.2) | collective-permute-done | bytes 229408 | tf_op jit(solution)/shard_map/ppermute | solution.py:19
  327.2 4.7 collective-permute-done.3
  333.0 16.4 %convolution_convert_fusion = bf16[14,256,1024]{2,1,0:T(8,128)(2,1)S(1)} fusion(f32[14,256,256]{2,1,0:T(8,128)S(1)} %fusion.27, f32[]{:T(128)S(6)} %sqrt.2, s32[256]{0:T(256)S(1)} %iota_multiply_fusion), kind=kOutput, calls=%fused_computation.9 | convolution fusion | flops 11282677760 | bytes 11011076 | tf_op jit(solution)/shard_map/brj,cj->brc/dot_general | solution.py:96
  349.5 7.5 %copy.32 = bf16[14,256,1024]{2,0,1:T(8,128)(2,1)} copy(bf16[14,256,1024]{2,1,0:T(8,128)(2,1)S(1)} %convolution_convert_fusion) | data formatting | bytes 14680064 | tf_op jit(solution)/shard_map/convert_element_type | solution.py:96
  357.0 5.3 %all-to-all-start.1 = ((bf16[14,256,1024]{2,0,1:T(8,128)(2,1)}), bf16[14,256,1024]{2,0,1:T(8,128)(2,1)}, u32[]{:S(2)}, u32[]{:S(2)}) async-start(bf16[14,256,1024]{2,0,1:T(8,128)(2,1)} %copy.32), calls=%async_computation.1 | async-start | bytes 16777216 | tf_op jit(solution)/shard_map/all_to_all | solution.py:99
  362.3 5.0 fusion.19
  367.2 89.9 %all-to-all-done.1 = bf16[14,256,1024]{2,0,1:T(8,128)(2,1)} async-done(((bf16[14,256,1024]{2,0,1:T(8,128)(2,1)}), bf16[14,256,1024]{2,0,1:T(8,128)(2,1)}, u32[]{:S(2)}, u32[]{:S(2)}) %all-to-all-start.1) | async-done | bytes 7340064 | tf_op jit(solution)/shard_map/all_to_all | solution.py:99
  457.1 7.5 %copy.33 = bf16[14,256,1024]{2,1,0:T(8,128)(2,1)S(1)} copy(bf16[14,256,1024]{2,0,1:T(8,128)(2,1)} %all-to-all-done.1) | data formatting | bytes 14680064 | tf_op jit(solution)/shard_map/all_to_all | solution.py:99
  464.6 7.1 %convert_bitcast_fusion = f32[16,14,16,1024]{3,2,0,1:T(8,128)} fusion(bf16[14,16,16,1024]{3,2,1,0:T(8,128)(2,1)S(1)} %bitcast.126), kind=kLoop, calls=%fused_computation.6 | loop fusion | flops 3670016 | bytes 22020096 | tf_op jit(solution)/shard_map/convert_element_type | solution.py:103
  471.7 13.7 %copy.34 = f32[16,14,16,1024]{3,2,1,0:T(8,128)} copy(f32[16,14,16,1024]{3,2,0,1:T(8,128)} %convert_bitcast_fusion) | data formatting | bytes 29360128 | tf_op jit(solution)/shard_map/convert_element_type | solution.py:103
  485.4 16.8 %fusion.11 = bf16[32,16,1024]{2,0,1:T(8,128)(2,1)S(1)} fusion(f32[224,16,1024]{2,1,0:T(8,128)} %bitcast.122, bf16[8,16,1024]{2,0,1:T(8,128)(2,1)S(1)} %fusion.19, bf16[32,16,1024]{2,1,0:T(8,128)(2,1)S(1)} %copy-done.3, bf16[224,32]{0,1:T(8,128)(2,1)S(1)} %copy-done, bf16[8,224]{1,0:T(8,128)(2,1)S(1)} %copy-done.6), kind=kOutput, calls=%fused_computation.16 | convolution fusion | flops 303038464 | bytes 17057280 | tf_op jit(solution)/shard_map/bk,brc->krc/dot_general | solution.py:104
  (40 shorter events, 22.4 us)
Async XLA Ops:
  0.6 0.7 copy-start
  4.7 15.2 %copy-start.1 = (bf16[224,16,1024]{2,0,1:T(8,128)(2,1)}, bf16[224,16,1024]{2,0,1:T(8,128)(2,1)S(1)}, u32[]{:S(2)}) copy-start(bf16[224,16,1024]{2,0,1:T(8,128)(2,1)S(1)} %convolution_convert_fusion.1) | copy-start | bytes 22020100
  123.6 3.0 copy-start.2
  131.0 87.0 %collective-permute-start = (bf16[14,128,1024]{2,1,0:T(8,128)(2,1)}, bf16[14,128,1024]{2,1,0:T(8,128)(2,1)}, u32[]{:S(2)}, u32[]{:S(2)}) collective-permute-start(bf16[14,128,1024]{2,1,0:T(8,128)(2,1)} %get-tuple-element.10), channel_id=1, source_target_pairs={{0,16},{16,32},{32,48},{48,64},{64,80},{80,96},{96,112},{112,128},... | collective-permute-start | bytes 11010056 | tf_op jit(solution)/shard_map/ppermute | solution.py:19
  136.1 158.0 %collective-permute-start.1 = (bf16[14,128,1024]{2,1,0:T(8,128)(2,1)}, bf16[14,128,1024]{2,1,0:T(8,128)(2,1)}, u32[]{:S(2)}, u32[]{:S(2)}) collective-permute-start(bf16[14,128,1024]{2,1,0:T(8,128)(2,1)} %get-tuple-element.11), channel_id=1, source_target_pairs={{16,0},{32,16},{48,32},{64,48},{80,64},{96,80},{112,96},{128,112},... | collective-permute-start | bytes 11010056 | tf_op jit(solution)/shard_map/ppermute | solution.py:21
  141.5 160.8 %copy-start.7 = (bf16[14,64,256]{2,1,0:T(8,128)(2,1)S(1)}, bf16[14,64,256]{2,1,0:T(8,128)(2,1)}, u32[]{:S(2)}) copy-start(bf16[14,64,256]{2,1,0:T(8,128)(2,1)} %param.8) | copy-start | bytes 1376260
  308.2 41.2 %copy-start.4 = (bf16[14,64,256]{2,1,0:T(8,128)(2,1)}, bf16[14,64,256]{2,1,0:T(8,128)(2,1)S(1)}, u32[]{:S(2)}) copy-start(bf16[14,64,256]{2,1,0:T(8,128)(2,1)S(1)} %fusion.15) | copy-start | bytes 1376260
  308.3 18.9 %collective-permute-start.2 = (bf16[14,32,256]{2,1,0:T(8,128)(2,1)S(1)}, bf16[14,32,256]{2,1,0:T(8,128)(2,1)S(1)}, u32[]{:S(2)}, u32[]{:S(2)}) collective-permute-start(bf16[14,32,256]{2,1,0:T(8,128)(2,1)S(1)} %get-tuple-element.12), channel_id=1, source_target_pairs={{0,16},{16,32},{32,48},{48,64},{64,80},{80,96},{96,112},{112,128},... | collective-permute-start | bytes 688136 | tf_op jit(solution)/shard_map/ppermute | solution.py:19
  319.6 12.3 %collective-permute-start.3 = (bf16[14,32,256]{2,1,0:T(8,128)(2,1)S(1)}, bf16[14,32,256]{2,1,0:T(8,128)(2,1)S(1)}, u32[]{:S(2)}, u32[]{:S(2)}) collective-permute-start(bf16[14,32,256]{2,1,0:T(8,128)(2,1)S(1)} %get-tuple-element.13), channel_id=1, source_target_pairs={{16,0},{32,16},{48,32},{64,48},{80,64},{96,80},{112,96},{128,112},... | collective-permute-start | bytes 688136 | tf_op jit(solution)/shard_map/ppermute | solution.py:21
  357.0 5.3 %copy-start.5 = (bf16[8,16,1024]{2,1,0:T(8,128)(2,1)S(1)}, bf16[8,16,1024]{2,1,0:T(8,128)(2,1)}, u32[]{:S(2)}) copy-start(bf16[8,16,1024]{2,1,0:T(8,128)(2,1)} %param.9) | copy-start | bytes 786436
  357.0 5.3 %copy-start.6 = (bf16[8,224]{1,0:T(8,128)(2,1)S(1)}, bf16[8,224]{1,0:T(8,128)(2,1)}, u32[]{:S(2)}) copy-start(bf16[8,224]{1,0:T(8,128)(2,1)} %param.7) | copy-start | bytes 10756
  357.0 100.2 %all-to-all-start.1 = ((bf16[14,256,1024]{2,0,1:T(8,128)(2,1)}), bf16[14,256,1024]{2,0,1:T(8,128)(2,1)}, u32[]{:S(2)}, u32[]{:S(2)}) async-start(bf16[14,256,1024]{2,0,1:T(8,128)(2,1)} %copy.32), calls=%async_computation.1 | async-start | bytes 16777216 | tf_op jit(solution)/shard_map/all_to_all | solution.py:99
  471.7 13.7 %copy-start.3 = (bf16[32,16,1024]{2,1,0:T(8,128)(2,1)S(1)}, bf16[32,16,1024]{2,1,0:T(8,128)(2,1)}, u32[]{:S(2)}) copy-start(bf16[32,16,1024]{2,1,0:T(8,128)(2,1)} %param.5) | copy-start | bytes 3145732
